TPU v7x, 256 devices: a whole 4x4x8 slice. The times are simulated.
256 devices in a mesh: seq: 64 (over z_hi, x, y, core), tp: 4 (over z_lo).
Axes of the slice: x: 4, y: 4, z: 8 (z_hi: 2, z_lo: 4; z = z_hi * 4 + z_lo), core: 2. Of those that a mesh axis runs over, the one named last changes fastest.
Arguments:
- query_rows: bfloat16 [16384, 4096], P('seq', 'tp'), may hold values from -6 to 6
- key_rows: bfloat16 [16384, 4096], P('seq', 'tp'), may hold values from -6 to 6
- value_rows: bfloat16 [16384, 4096], P('seq', 'tp'), may hold values from -6 to 6
- short_filter: float32 [3, 3, 4096], P(None, None, 'tp'), may hold values from -3 to 3
- long_filter: bfloat16 [16384, 4096], P('seq', 'tp'), may hold values from -1.1 to 1.1, as said below
- skip_gain: float32 [4096], P('tp'), may hold values from -4 to 4
- out_weight: bfloat16 [4096, 4096], P('seq', 'tp'), may hold values from -0.09375 to 0.09375
Outputs:
- projected: bfloat16 [16384, 4096], P('seq', 'tp')
Inputs may be any that keep to these rules, and one draw needn't show every extreme that they name: `long_filter`: taps of the long filter.
All inputs are finite; a program needn't handle non-finite values.
Results may differ from a plain program's by a relative error of at most 0.0061.
Values may be sent and summed in bfloat16 or wider, within the bound.
No kernel may reach another device: no remote copies, remote signals or barrier semaphores. Data moves between devices by JAX's collectives and lax.ppermute only.
A program may use at most 64 MiB of HBM per device.

v0:
```python
import math
import numpy as np
import jax
import jax.numpy as jnp
from jax import lax
from jax.sharding import PartitionSpec as P

TRANSFORM_PRECISION = lax.Precision.HIGH


def shifted(value, axis, by):
    size = lax.axis_size(axis)
    pairs = [(i, i + by) for i in range(size) if 0 <= i + by < size]
    return lax.ppermute(value, axis, pairs)


def make_tables(blocks, tokens):
    outer = 2 * blocks
    period = outer * tokens
    k1 = np.arange(outer, dtype=np.int64)
    n1 = np.arange(blocks, dtype=np.int64)
    n2 = np.arange(tokens, dtype=np.int64)
    first = 2.0 * np.pi * (k1[:, None] * n1[None, :] % outer) / outer
    first_table = np.concatenate([np.cos(first), -np.sin(first)], 0)
    twist = 2.0 * np.pi * (k1[:, None] * n2[None, :] % period) / period
    twist_cos = np.cos(twist)[:, None, :]
    twist_sin = np.sin(twist)[:, None, :]
    inner = 2.0 * np.pi * (n2[:, None] * n2[None, :] % tokens) / tokens
    b_cos = np.cos(inner)
    b_sin = np.sin(inner)
    forward = np.block([[b_cos, -b_sin], [b_sin, b_cos]])
    backward = np.block([[b_cos, b_sin], [-b_sin, b_cos]])
    last = 2.0 * np.pi * (n1[:, None] * k1[None, :] % outer) / outer
    last_table = np.concatenate([np.cos(last), -np.sin(last)], 1) / period
    as32 = lambda a: jnp.asarray(a, jnp.float32)
    return tuple(
        (as32(a) for a in (first_table, twist_cos, twist_sin, forward, backward, last_table))
    )


def dot(a, b):
    return jnp.dot(a, b, precision=TRANSFORM_PRECISION, preferred_element_type=jnp.float32)


def long_conv(pieces, per_device, tables):
    first_table, twist_cos, twist_sin, forward, backward, last_table = tables
    blocks, both, tokens = pieces.shape
    outer = 2 * blocks
    spec = dot(first_table, pieces.reshape(blocks, both * tokens)).reshape(2, outer, both, tokens)
    s_real, s_imag = (spec[0], spec[1])
    w_real = s_real * twist_cos + s_imag * twist_sin
    w_imag = s_imag * twist_cos - s_real * twist_sin
    twisted = jnp.concatenate([w_real, w_imag], -1).reshape(outer * both, 2 * tokens)
    u = dot(twisted, forward).reshape(outer, both, 2 * tokens)
    u_real, u_imag = (u[:, :per_device, :tokens], u[:, :per_device, tokens:])
    f_real, f_imag = (u[:, per_device:, :tokens], u[:, per_device:, tokens:])
    p_real = u_real * f_real - u_imag * f_imag
    p_imag = u_real * f_imag + u_imag * f_real
    product = jnp.concatenate([p_real, p_imag], -1).reshape(outer * per_device, 2 * tokens)
    q = dot(product, backward).reshape(outer, per_device, 2 * tokens)
    q_real, q_imag = (q[..., :tokens], q[..., tokens:])
    r_real = q_real * twist_cos - q_imag * twist_sin
    r_imag = q_real * twist_sin + q_imag * twist_cos
    stacked = jnp.stack([r_real, r_imag], 0).reshape(2 * outer, per_device * tokens)
    result = dot(last_table, stacked)
    return result.reshape(blocks, per_device, tokens).astype(jnp.bfloat16)


def causal_short(rows, tail, taps):
    extended = jnp.concatenate([tail, rows], 0)
    return (
        taps[0] * extended[2:].astype(jnp.float32)
        + taps[1] * extended[1:-1].astype(jnp.float32)
        + taps[2] * extended[:-2].astype(jnp.float32)
    )


def body(query_rows, key_rows, value_rows, short_filter, long_filter, skip_gain, out_weight):
    tokens_here, channels = query_rows.shape
    groups = lax.axis_size("seq")
    per_device = channels // groups
    tables = make_tables(groups, tokens_here)
    tails = shifted((query_rows[-2:], key_rows[-2:], value_rows[-2:]), "seq", 1)
    query_mix = causal_short(query_rows, tails[0], short_filter[:, 0, :])
    key_mix = causal_short(key_rows, tails[1], short_filter[:, 1, :])
    value_mix = causal_short(value_rows, tails[2], short_filter[:, 2, :])
    gated = (key_mix * value_mix).astype(jnp.bfloat16)
    gated_cols = gated.T.reshape(groups, per_device, tokens_here)
    filter_cols = long_filter.T.reshape(groups, per_device, tokens_here)
    outgoing = jnp.concatenate([gated_cols, filter_cols], 1)
    pieces = lax.all_to_all(outgoing, "seq", split_axis=0, concat_axis=0, tiled=True)
    mixed = long_conv(pieces, per_device, tables)
    returned = lax.all_to_all(mixed, "seq", split_axis=0, concat_axis=0, tiled=True)
    conv = returned.reshape(channels, tokens_here).T
    inner = (query_mix * (conv.astype(jnp.float32) + skip_gain * gated.astype(jnp.float32))).astype(
        jnp.bfloat16
    )
    weights = lax.all_gather(out_weight, "seq", axis=0, tiled=True)
    total = jnp.dot(
        lax.all_gather(inner, "tp", axis=1, tiled=True), weights, preferred_element_type=jnp.float32
    )
    return total.astype(jnp.bfloat16)


def solution(mesh):
    placed = (
        P("seq", "tp"),
        P("seq", "tp"),
        P("seq", "tp"),
        P(None, None, "tp"),
        P("seq", "tp"),
        P("tp"),
        P("seq", "tp"),
    )
    return jax.shard_map(
        body, mesh=mesh, in_specs=placed, out_specs=P("seq", "tp"), check_vma=False
    )
```

profile of v0, /device:TPU:1, one launch (start us, length us, event | category | flops | bytes accessed | tf_op | source)
XLA Modules:
  0.0 303.2 jit_solution(137879276982766816)
XLA Ops:
  6.5 0.7 slice.109
  7.3 0.2 copy.23
  7.5 4.6 %collective-permute-start.1 = (bf16[2,1024]{0,1:T(8,128)(2,1)S(1)}, bf16[2,1024]{0,1:T(8,128)(2,1)S(1)}, u32[]{:S(2)}, u32[]{:S(2)}) collective-permute-start(bf16[2,1024]{0,1:T(8,128)(2,1)S(1)} %copy.23), channel_id=1, source_target_pairs={{0,4},{4,8},{8,12},{12,16},{16,20},{20,24},{24,28},{28,32},{32,36}... | collective-permute-start | bytes 12296 | tf_op jit(solution)/shard_map/ppermute | solution.py:14
  12.1 0.7 slice.115
  12.8 0.2 copy.26
  13.0 1.9 collective-permute-start.2
  14.9 0.9 fusion.19
  15.8 1.2 copy.22
  17.1 1.2 copy.25
  18.3 1.2 copy.28
  19.6 0.0 collective-permute-done.1
  19.6 0.0 collective-permute-done.2
  19.6 0.0 copy-start.5
  19.6 1.9 multiply_convert_fusion
  21.5 0.1 pad_maximum_fusion.1
  21.6 38.1 %all_to_all.10 = bf16[64,32,256]{2,1,0:T(8,128)(2,1)S(1)} all-to-all(bf16[64,32,256]{2,1,0:T(8,128)(2,1)S(1)} %pad_maximum_fusion.1), channel_id=1, replica_groups=mesh['seq'=64,'tp'=4] {'seq'}, dimensions={0} | all-to-all | bytes 2097152 | tf_op jit(solution)/shard_map/all_to_all | solution.py:91
  59.7 0.6 copy.36
  60.4 0.0 copy-done.5
  60.4 2.3 fusion.20
  62.7 0.0 copy-start.3
  62.7 0.0 copy-start.4
  62.7 0.6 fusion.18
  63.3 0.3 copy-done.3
  63.6 0.1 copy-done.4
  63.7 0.0 copy-start.1
  63.7 1.2 fusion.4
  64.9 0.0 copy-done.1
  64.9 7.0 %fusion = f32[128,32,512]{2,0,1:T(8,128)S(1)} fusion(f32[512,512,1]{1,0,2:T(8,128)S(1)} %copy-done.1, f32[128,32,256]{2,0,1:T(8,128)S(1)} %get-tuple-element.6, f32[128,32,256]{2,0,1:T(8,128)S(1)} %get-tuple-element.5), kind=kOutput, calls=%fused_computation | convolution fusion | flops 6444548096 | bytes 17825792 | tf_op jit(solution)/shard_map/dot_general | solution.py:42
  72.0 0.0 copy-start
  72.0 0.8 multiply_subtract_fusion
  72.8 0.4 copy-done
  73.2 3.5 %fusion.6 = f32[128,16,512]{2,0,1:T(8,128)S(1)} fusion(f32[512,512,1]{1,0,2:T(8,128)S(1)} %copy-done, f32[128,16,256]{2,0,1:T(8,128)S(1)} %get-tuple-element.8, f32[128,16,256]{2,0,1:T(8,128)S(1)} %get-tuple-element.7), kind=kOutput, calls=%fused_computation.11 | convolution fusion | flops 3222274048 | bytes 9437184 | tf_op jit(solution)/shard_map/dot_general | solution.py:42
  76.7 0.6 subtract_bitcast_fusion
  77.4 0.4 pad_maximum_fusion
  77.7 2.4 copy.33
  80.2 0.0 copy-start.6
  80.2 3.8 %copy.37 = f32[32,8,16,256]{3,1,2,0:T(8,128)S(1)} copy(f32[32,8,16,256]{3,2,1,0:T(8,128)S(1)} %bitcast.65) | data formatting | bytes 8388608
  84.0 0.0 copy-start.2
  84.0 0.0 copy-start.7
  84.0 0.0 copy-done.6
  84.0 1.4 convolution_convert_fusion
  85.4 1.2 copy.38
  86.5 15.5 %all-to-all-start.1 = ((bf16[64,16,256]{2,1,0:T(8,128)(2,1)}), bf16[64,16,256]{2,1,0:T(8,128)(2,1)S(1)}, u32[]{:S(2)}, u32[]{:S(2)}) async-start(bf16[64,16,256]{2,1,0:T(8,128)(2,1)} %bitcast.33), calls=%async_computation.1 | async-start | bytes 1048576 | tf_op jit(solution)/shard_map/all_to_all | solution.py:93
  102.0 0.0 all-gather.3.cloned.1.call-start
  102.0 0.0 copy-done.2
  102.1 0.2 copy.20
  102.3 3.5 %collective-permute-start = (bf16[2,1024]{0,1:T(8,128)(2,1)S(1)}, bf16[2,1024]{0,1:T(8,128)(2,1)S(1)}, u32[]{:S(2)}, u32[]{:S(2)}) collective-permute-start(bf16[2,1024]{0,1:T(8,128)(2,1)S(1)} %copy.20), channel_id=1, source_target_pairs={{0,4},{4,8},{8,12},{12,16},{16,20},{20,24},{24,28},{28,32},{32,36}... | collective-permute-start | bytes 12296 | tf_op jit(solution)/shard_map/ppermute | solution.py:14
  105.8 0.2 copy.19
  106.0 4.8 %collective-permute-done = bf16[2,1024]{0,1:T(8,128)(2,1)S(1)} collective-permute-done((bf16[2,1024]{0,1:T(8,128)(2,1)S(1)}, bf16[2,1024]{0,1:T(8,128)(2,1)S(1)}, u32[]{:S(2)}, u32[]{:S(2)}) %collective-permute-start) | collective-permute-done | bytes 4128 | tf_op jit(solution)/shard_map/ppermute | solution.py:14
  110.8 11.9 %all-to-all-done.1 = bf16[64,16,256]{2,1,0:T(8,128)(2,1)S(1)} async-done(((bf16[64,16,256]{2,1,0:T(8,128)(2,1)}), bf16[64,16,256]{2,1,0:T(8,128)(2,1)S(1)}, u32[]{:S(2)}, u32[]{:S(2)}) %all-to-all-start.1) | async-done | bytes 524320 | tf_op jit(solution)/shard_map/all_to_all | solution.py:93
  122.7 0.0 copy-done.7
  122.7 1.9 fusion.12
  124.6 0.0 all-gather.3.cloned.1.call-update
  124.6 0.0 all-gather.5.cloned.1.call-start
  124.7 0.7 all-gather.5.cloned.1.call-update
  125.4 47.1 %all-gather.3.cloned.1.call-done = bf16[256,4096]{0,1:T(8,128)(2,1)} async-done(((bf16[256,1024]{0,1:T(8,128)(2,1)}), bf16[256,4096]{0,1:T(8,128)(2,1)}) %all-gather.3.cloned.1.call-update) | async-done | bytes 2097168 | tf_op jit(solution)/shard_map/all_gather | solution.py:100
  172.5 116.6 %all-gather.5.cloned.1.call-done = bf16[4096,1024]{1,0:T(8,128)(2,1)} async-done(((bf16[64,1024]{1,0:T(8,128)(2,1)}), bf16[4096,1024]{1,0:T(8,128)(2,1)}) %all-gather.5.cloned.1.call-update) | async-done | bytes 8388624 | tf_op jit(solution)/shard_map/all_gather | solution.py:98
  289.1 7.2 %convolution_convert_fusion.1 = bf16[256,1024]{1,0:T(8,128)(2,1)} fusion(bf16[256,4096]{0,1:T(8,128)(2,1)} %all-gather.3.cloned.1.call-done, bf16[4096,1024]{1,0:T(8,128)(2,1)} %all-gather.5.cloned.1.call-done), kind=kOutput, calls=%fused_computation.20 | convolution fusion | flops 2147745792 | bytes 11010048 | tf_op jit(solution)/shard_map/dot_general | solution.py:99
  (1 shorter events, 0.0 us)
Async XLA Ops:
  7.5 12.1 %collective-permute-start.1 = (bf16[2,1024]{0,1:T(8,128)(2,1)S(1)}, bf16[2,1024]{0,1:T(8,128)(2,1)S(1)}, u32[]{:S(2)}, u32[]{:S(2)}) collective-permute-start(bf16[2,1024]{0,1:T(8,128)(2,1)S(1)} %copy.23), channel_id=1, source_target_pairs={{0,4},{4,8},{8,12},{12,16},{16,20},{20,24},{24,28},{28,32},{32,36}... | collective-permute-start | bytes 12296 | tf_op jit(solution)/shard_map/ppermute | solution.py:14
  13.0 6.6 %collective-permute-start.2 = (bf16[2,1024]{0,1:T(8,128)(2,1)S(1)}, bf16[2,1024]{0,1:T(8,128)(2,1)S(1)}, u32[]{:S(2)}, u32[]{:S(2)}) collective-permute-start(bf16[2,1024]{0,1:T(8,128)(2,1)S(1)} %copy.26), channel_id=1, source_target_pairs={{0,4},{4,8},{8,12},{12,16},{16,20},{20,24},{24,28},{28,32},{32,36}... | collective-permute-start | bytes 12296 | tf_op jit(solution)/shard_map/ppermute | solution.py:14
  19.6 40.8 %copy-start.5 = (f32[256,64]{1,0:T(8,128)S(1)}, f32[256,64]{1,0:T(8,128)}, u32[]{:S(2)}) copy-start(f32[256,64]{1,0:T(8,128)} %constant.12.clone) | copy-start | bytes 196612
  62.7 0.9 copy-start.3
  62.7 1.0 copy-start.4
  63.7 1.3 copy-start.1
  72.0 1.2 copy-start
  80.2 3.8 %copy-start.6 = (f32[64,256]{1,0:T(8,128)S(1)}, f32[64,256]{1,0:T(8,128)}, u32[]{:S(2)}) copy-start(f32[64,256]{1,0:T(8,128)} %constant.17.clone) | copy-start | bytes 196612
  84.0 18.1 %copy-start.2 = (bf16[256,1024]{1,0:T(8,128)(2,1)S(1)}, bf16[256,1024]{1,0:T(8,128)(2,1)}, u32[]{:S(2)}) copy-start(bf16[256,1024]{1,0:T(8,128)(2,1)} %param.13) | copy-start | bytes 1572868
  84.0 38.7 %copy-start.7 = (f32[1024]{0:T(1024)S(1)}, f32[1024]{0:T(1024)}, u32[]{:S(2)}) copy-start(f32[1024]{0:T(1024)} %param.18) | copy-start | bytes 12292
  86.5 36.2 %all-to-all-start.1 = ((bf16[64,16,256]{2,1,0:T(8,128)(2,1)}), bf16[64,16,256]{2,1,0:T(8,128)(2,1)S(1)}, u32[]{:S(2)}, u32[]{:S(2)}) async-start(bf16[64,16,256]{2,1,0:T(8,128)(2,1)} %bitcast.33), calls=%async_computation.1 | async-start | bytes 1048576 | tf_op jit(solution)/shard_map/all_to_all | solution.py:93
  102.0 70.5 %all-gather.3.cloned.1.call-start = ((), (), s32[]{:S(2)}) async-start(), calls=%async_computation.2 | async-start | bytes 2621440 | tf_op jit(solution)/shard_map/all_gather | solution.py:100
  102.3 8.5 %collective-permute-start = (bf16[2,1024]{0,1:T(8,128)(2,1)S(1)}, bf16[2,1024]{0,1:T(8,128)(2,1)S(1)}, u32[]{:S(2)}, u32[]{:S(2)}) collective-permute-start(bf16[2,1024]{0,1:T(8,128)(2,1)S(1)} %copy.20), channel_id=1, source_target_pairs={{0,4},{4,8},{8,12},{12,16},{16,20},{20,24},{24,28},{28,32},{32,36}... | collective-permute-start | bytes 12296 | tf_op jit(solution)/shard_map/ppermute | solution.py:14
  124.6 164.5 %all-gather.5.cloned.1.call-start = ((), (), s32[]{:S(2)}) async-start(), calls=%async_computation.3 | async-start | bytes 8519680 | tf_op jit(solution)/shard_map/all_gather | solution.py:98
Sparse Core Ops, SparseCore 0:
  124.8 47.7 all-gather.2
  176.1 112.9 all-gather.4
where the time goes:
time: 304 us; the launch traced here: 303 us
  waiting for transfers between devices  181 us (60%)
  blocking collectives  38.1 us (13%)
  starting transfers between devices  25.6 us (8%)
  matrix products  21.4 us (7%)
  local copies, waits for them, and re-layouts  16.3 us (5%)
  between operations  13.7 us (5%)
  other arithmetic  6.97 us (2%)
    all_gather x1, waiting for transfers between devices, body(): weights = lax.all_gather(out_weight, 'seq', axis=0, tiled=True)  117 us
    all_gather x1, waiting for transfers between devices, body(): lax.all_gather(inner, 'tp', axis=1, tiled=True)  47.1 us
    all_to_all x1, blocking collectives, body(): lax.all_to_all(outgoing, 'seq', split_axis=0, concat_axis=0, tiled=True)  38.1 us
    all_to_all x1, starting transfers between devices, body(): lax.all_to_all(mixed, 'seq', split_axis=0, concat_axis=0, tiled=True)  15.5 us
    dot_general x4, matrix products, dot(): jnp.dot(a, b, precision=TRANSFORM_PRECISION, preferred_element_type=jnp.f...  14.2 us
    all_to_all x1, waiting for transfers between devices, body(): lax.all_to_all(mixed, 'seq', split_axis=0, concat_axis=0, tiled=True)  11.9 us
    unnamed x23, local copies, waits for them, and re-layouts  10.3 us
    ppermute x3, starting transfers between devices, shifted(): return lax.ppermute(value, axis, pairs)  10 us
  transfers between devices with their start and end apart: 6, of which 4 were waited for; matrix products, arithmetic and copies ran while one was open for 2% of the time, Pallas kernels for 0%

commit v1 on v0

--- a/solution.py
+++ b/solution.py
@@ -97,7 +97,11 @@
     )
     weights = lax.all_gather(out_weight, "seq", axis=0, tiled=True)
     total = jnp.dot(
-        lax.all_gather(inner, "tp", axis=1, tiled=True), weights, preferred_element_type=jnp.float32
+        jnp.concatenate(
+            lax.all_to_all(jnp.stack([inner] * lax.axis_size("tp")), "tp", 0, 0), axis=1
+        ),
+        weights,
+        preferred_element_type=jnp.float32,
     )
     return total.astype(jnp.bfloat16)
 

time: 304 us -> 209 us (0.69)
  waiting for transfers between devices: 181 us -> 31.6 us
  blocking collectives: 38.1 us -> 88.3 us
  starting transfers between devices: 25.6 us -> 29.6 us
    all_gather x1, waiting for transfers between devices: 117 us -> 0.01 us  [body(): weights = lax.all_gather(out_weight, 'seq', axis=0, tiled=True)]
    all_to_all x0 -> x1, blocking collectives: none -> 50.2 us  [body(): lax.all_to_all(jnp.stack([inner] * lax.axis_size('tp')), 'tp', 0, 0)]
    all_gather x1 -> x0, waiting for transfers between devices: 47.1 us -> none  [body(): lax.all_gather(inner, 'tp', axis=1, tiled=True)]
    all_to_all x1, waiting for transfers between devices: 11.9 us -> 25.8 us  [body(): lax.all_to_all(mixed, 'seq', split_axis=0, concat_axis=0, tiled=True)]
    all_to_all x1, starting transfers between devices: 15.5 us -> 19.5 us  [body(): lax.all_to_all(mixed, 'seq', split_axis=0, concat_axis=0, tiled=True)]
  transfers between devices with their start and end apart: 6 -> 5, of which waited for: 4 -> 2; matrix products, arithmetic and copies ran while one was open for 2% -> 17% of each run, Pallas kernels for 0% -> 0%
where the time goes in v1:
time: 209 us; the launch traced here: 207 us
  blocking collectives  88.3 us (42%)
  waiting for transfers between devices  31.6 us (15%)
  starting transfers between devices  29.6 us (14%)
  matrix products  20.7 us (10%)
  local copies, waits for them, and re-layouts  16.5 us (8%)
  between operations  13.7 us (7%)
  other arithmetic  6.28 us (3%)
    all_to_all x1, blocking collectives, body(): lax.all_to_all(jnp.stack([inner] * lax.axis_size('tp')), 'tp', 0, 0)  50.2 us
    all_to_all x1, blocking collectives, body(): lax.all_to_all(outgoing, 'seq', split_axis=0, concat_axis=0, tiled=True)  38.1 us
    all_to_all x1, waiting for transfers between devices, body(): lax.all_to_all(mixed, 'seq', split_axis=0, concat_axis=0, tiled=True)  25.8 us
    all_to_all x1, starting transfers between devices, body(): lax.all_to_all(mixed, 'seq', split_axis=0, concat_axis=0, tiled=True)  19.5 us
    dot_general x4, matrix products, dot(): jnp.dot(a, b, precision=TRANSFORM_PRECISION, preferred_element_type=jnp.f...  14.2 us
    unnamed x23, local copies, waits for them, and re-layouts  10.3 us
    ppermute x3, starting transfers between devices, shifted(): return lax.ppermute(value, axis, pairs)  10 us
    dot_general x1, matrix products, body(): jnp.dot(jnp.concatenate(lax.all_to_all(jnp.stack([inner] * lax.axis_size(...  6.53 us
  transfers between devices with their start and end apart: 5, of which 2 were waited for; matrix products, arithmetic and copies ran while one was open for 17% of the time, Pallas kernels for 0%

profile of v1, /device:TPU:1, one launch (start us, length us, event | category | flops | bytes accessed | tf_op | source)
XLA Modules:
  0.0 206.7 jit_solution(13400174672225979225)
XLA Ops:
  6.5 0.0 all-gather.2.cloned.1.call-start
  6.5 0.7 all-gather.2.cloned.1.call-update
  7.3 0.7 slice.109
  8.0 0.2 copy.23
  8.2 4.6 %collective-permute-start.1 = (bf16[2,1024]{0,1:T(8,128)(2,1)S(1)}, bf16[2,1024]{0,1:T(8,128)(2,1)S(1)}, u32[]{:S(2)}, u32[]{:S(2)}) collective-permute-start(bf16[2,1024]{0,1:T(8,128)(2,1)S(1)} %copy.23), channel_id=1, source_target_pairs={{0,4},{4,8},{8,12},{12,16},{16,20},{20,24},{24,28},{28,32},{32,36}... | collective-permute-start | bytes 12296 | tf_op jit(solution)/shard_map/ppermute | solution.py:14
  12.8 0.7 slice.115
  13.5 0.2 copy.26
  13.7 1.9 collective-permute-start.2
  15.6 0.9 fusion.19
  16.6 1.2 copy.22
  17.8 1.2 copy.25
  19.1 1.2 copy.28
  20.3 0.0 collective-permute-done.1
  20.3 0.0 collective-permute-done.2
  20.3 0.0 copy-start.5
  20.4 1.9 multiply_convert_fusion
  22.3 0.1 pad_maximum_fusion.1
  22.4 38.1 %all_to_all.15 = bf16[64,32,256]{2,1,0:T(8,128)(2,1)S(1)} all-to-all(bf16[64,32,256]{2,1,0:T(8,128)(2,1)S(1)} %pad_maximum_fusion.1), channel_id=1, replica_groups=mesh['seq'=64,'tp'=4] {'seq'}, dimensions={0} | all-to-all | bytes 2097152 | tf_op jit(solution)/shard_map/all_to_all | solution.py:91
  60.5 0.6 copy.36
  61.1 0.0 copy-done.5
  61.1 2.3 %fusion.20 = f32[256,8192]{1,0:T(8,128)S(1)} fusion(f32[256,64]{1,0:T(8,128)S(1)} %copy-done.5, bf16[64,8192]{1,0:T(8,128)(2,1)S(1)} %bitcast.73), kind=kOutput, calls=%fused_computation.43 | convolution fusion | flops 805306368 | bytes 9502720 | tf_op jit(solution)/shard_map/dot_general | solution.py:42
  63.4 0.0 copy-start.3
  63.4 0.0 copy-start.4
  63.5 0.6 fusion.18
  64.1 0.3 copy-done.3
  64.3 0.1 copy-done.4
  64.4 0.0 copy-start.1
  64.4 1.2 fusion.4
  65.7 0.0 copy-done.1
  65.7 7.0 %fusion = f32[128,32,512]{2,0,1:T(8,128)S(1)} fusion(f32[512,512,1]{1,0,2:T(8,128)S(1)} %copy-done.1, f32[128,32,256]{2,0,1:T(8,128)S(1)} %get-tuple-element.6, f32[128,32,256]{2,0,1:T(8,128)S(1)} %get-tuple-element.5), kind=kOutput, calls=%fused_computation | convolution fusion | flops 6444548096 | bytes 17825792 | tf_op jit(solution)/shard_map/dot_general | solution.py:42
  72.7 0.0 copy-start
  72.7 0.8 multiply_subtract_fusion
  73.5 0.4 copy-done
  74.0 3.5 %fusion.6 = f32[128,16,512]{2,0,1:T(8,128)S(1)} fusion(f32[512,512,1]{1,0,2:T(8,128)S(1)} %copy-done, f32[128,16,256]{2,0,1:T(8,128)S(1)} %get-tuple-element.8, f32[128,16,256]{2,0,1:T(8,128)S(1)} %get-tuple-element.7), kind=kOutput, calls=%fused_computation.11 | convolution fusion | flops 3222274048 | bytes 9437184 | tf_op jit(solution)/shard_map/dot_general | solution.py:42
  77.4 0.6 subtract_bitcast_fusion
  78.1 0.4 pad_maximum_fusion
  78.5 2.4 %copy.33 = f32[2,128,16,256]{3,2,1,0:T(8,128)S(1)} copy(f32[2,128,16,256]{3,1,2,0:T(8,128)S(1)} %pad_maximum_fusion) | data formatting | bytes 8388608 | tf_op jit(solution)/shard_map/stack | solution.py:64
  80.9 0.0 copy-start.6
  80.9 3.8 %copy.37 = f32[32,8,16,256]{3,1,2,0:T(8,128)S(1)} copy(f32[32,8,16,256]{3,2,1,0:T(8,128)S(1)} %bitcast.68) | data formatting | bytes 8388608
  84.7 0.0 copy-start.2
  84.7 0.0 copy-start.7
  84.7 0.0 copy-done.6
  84.7 1.3 convolution_convert_fusion
  86.1 1.2 copy.38
  87.2 19.5 %all-to-all-start.1 = ((bf16[64,16,256]{2,1,0:T(8,128)(2,1)}), bf16[64,16,256]{2,1,0:T(8,128)(2,1)S(1)}, u32[]{:S(2)}, u32[]{:S(2)}) async-start(bf16[64,16,256]{2,1,0:T(8,128)(2,1)} %bitcast.36), calls=%async_computation.1 | async-start | bytes 1048576 | tf_op jit(solution)/shard_map/all_to_all | solution.py:93
  106.8 0.0 copy-done.2
  106.8 0.2 copy.20
  107.0 3.5 %collective-permute-start = (bf16[2,1024]{0,1:T(8,128)(2,1)S(1)}, bf16[2,1024]{0,1:T(8,128)(2,1)S(1)}, u32[]{:S(2)}, u32[]{:S(2)}) collective-permute-start(bf16[2,1024]{0,1:T(8,128)(2,1)S(1)} %copy.20), channel_id=1, source_target_pairs={{0,4},{4,8},{8,12},{12,16},{16,20},{20,24},{24,28},{28,32},{32,36}... | collective-permute-start | bytes 12296 | tf_op jit(solution)/shard_map/ppermute | solution.py:14
  110.6 0.2 copy.19
  110.8 5.0 %collective-permute-done = bf16[2,1024]{0,1:T(8,128)(2,1)S(1)} collective-permute-done((bf16[2,1024]{0,1:T(8,128)(2,1)S(1)}, bf16[2,1024]{0,1:T(8,128)(2,1)S(1)}, u32[]{:S(2)}, u32[]{:S(2)}) %collective-permute-start) | collective-permute-done | bytes 4128 | tf_op jit(solution)/shard_map/ppermute | solution.py:14
  115.8 25.8 %all-to-all-done.1 = bf16[64,16,256]{2,1,0:T(8,128)(2,1)S(1)} async-done(((bf16[64,16,256]{2,1,0:T(8,128)(2,1)}), bf16[64,16,256]{2,1,0:T(8,128)(2,1)S(1)}, u32[]{:S(2)}, u32[]{:S(2)}) %all-to-all-start.1) | async-done | bytes 524320 | tf_op jit(solution)/shard_map/all_to_all | solution.py:93
  141.7 0.0 copy-done.7
  141.7 1.3 fusion.12
  142.9 0.1 stack.19
  143.1 50.2 %all_to_all.16 = bf16[4,256,1024]{1,2,0:T(8,128)(2,1)S(1)} all-to-all(bf16[4,256,1024]{1,2,0:T(8,128)(2,1)S(1)} %stack.19), channel_id=1, replica_groups=mesh['seq'=64,'tp'=4] {'tp'}, dimensions={0} | all-to-all | bytes 4194304 | tf_op jit(solution)/shard_map/all_to_all | solution.py:101
  193.3 0.0 all-gather.2.cloned.1.call-done
  193.3 6.5 %convolution_convert_fusion.1 = bf16[256,1024]{1,0:T(8,128)(2,1)} fusion(bf16[256,4096]{0,1:T(8,128)(2,1)S(1)} %bitcast.71, bf16[4096,1024]{1,0:T(8,128)(2,1)} %all-gather.2.cloned.1.call-done), kind=kOutput, calls=%fused_computation.20 | convolution fusion | flops 2147745792 | bytes 11010048 | tf_op jit(solution)/shard_map/dot_general | solution.py:99
  (1 shorter events, 0.0 us)
Async XLA Ops:
  6.5 186.7 %all-gather.2.cloned.1.call-start = ((), (), s32[]{:S(2)}) async-start(), calls=%async_computation.3 | async-start | bytes 8519680 | tf_op jit(solution)/shard_map/all_gather | solution.py:98
  8.2 12.1 %collective-permute-start.1 = (bf16[2,1024]{0,1:T(8,128)(2,1)S(1)}, bf16[2,1024]{0,1:T(8,128)(2,1)S(1)}, u32[]{:S(2)}, u32[]{:S(2)}) collective-permute-start(bf16[2,1024]{0,1:T(8,128)(2,1)S(1)} %copy.23), channel_id=1, source_target_pairs={{0,4},{4,8},{8,12},{12,16},{16,20},{20,24},{24,28},{28,32},{32,36}... | collective-permute-start | bytes 12296 | tf_op jit(solution)/shard_map/ppermute | solution.py:14
  13.7 6.6 %collective-permute-start.2 = (bf16[2,1024]{0,1:T(8,128)(2,1)S(1)}, bf16[2,1024]{0,1:T(8,128)(2,1)S(1)}, u32[]{:S(2)}, u32[]{:S(2)}) collective-permute-start(bf16[2,1024]{0,1:T(8,128)(2,1)S(1)} %copy.26), channel_id=1, source_target_pairs={{0,4},{4,8},{8,12},{12,16},{16,20},{20,24},{24,28},{28,32},{32,36}... | collective-permute-start | bytes 12296 | tf_op jit(solution)/shard_map/ppermute | solution.py:14
  20.3 40.8 %copy-start.5 = (f32[256,64]{1,0:T(8,128)S(1)}, f32[256,64]{1,0:T(8,128)}, u32[]{:S(2)}) copy-start(f32[256,64]{1,0:T(8,128)} %constant.12.clone) | copy-start | bytes 196612
  63.4 0.9 copy-start.3
  63.4 1.0 copy-start.4
  64.4 1.3 copy-start.1
  72.7 1.2 copy-start
  80.9 3.8 %copy-start.6 = (f32[64,256]{1,0:T(8,128)S(1)}, f32[64,256]{1,0:T(8,128)}, u32[]{:S(2)}) copy-start(f32[64,256]{1,0:T(8,128)} %constant.17.clone) | copy-start | bytes 196612
  84.7 22.1 %copy-start.2 = (bf16[256,1024]{1,0:T(8,128)(2,1)S(1)}, bf16[256,1024]{1,0:T(8,128)(2,1)}, u32[]{:S(2)}) copy-start(bf16[256,1024]{1,0:T(8,128)(2,1)} %param.13) | copy-start | bytes 1572868
  84.7 56.9 %copy-start.7 = (f32[1024]{0:T(1024)S(1)}, f32[1024]{0:T(1024)}, u32[]{:S(2)}) copy-start(f32[1024]{0:T(1024)} %param.18) | copy-start | bytes 12292
  87.2 54.4 %all-to-all-start.1 = ((bf16[64,16,256]{2,1,0:T(8,128)(2,1)}), bf16[64,16,256]{2,1,0:T(8,128)(2,1)S(1)}, u32[]{:S(2)}, u32[]{:S(2)}) async-start(bf16[64,16,256]{2,1,0:T(8,128)(2,1)} %bitcast.36), calls=%async_computation.1 | async-start | bytes 1048576 | tf_op jit(solution)/shard_map/all_to_all | solution.py:93
  107.0 8.8 %collective-permute-start = (bf16[2,1024]{0,1:T(8,128)(2,1)S(1)}, bf16[2,1024]{0,1:T(8,128)(2,1)S(1)}, u32[]{:S(2)}, u32[]{:S(2)}) collective-permute-start(bf16[2,1024]{0,1:T(8,128)(2,1)S(1)} %copy.20), channel_id=1, source_target_pairs={{0,4},{4,8},{8,12},{12,16},{16,20},{20,24},{24,28},{28,32},{32,36}... | collective-permute-start | bytes 12296 | tf_op jit(solution)/shard_map/ppermute | solution.py:14
Sparse Core Ops, SparseCore 0:
  10.9 141.8 all-gather.1
